TPU v7x, 256 devices: a whole 4x4x8 slice. The times are simulated.
256 devices in a mesh: dp: 16 (over x_hi, y, core), block: 16 (over z, x_lo).
Axes of the slice: x: 4 (x_hi: 2, x_lo: 2; x = x_hi * 2 + x_lo), y: 4, z: 8, core: 2. Of those that a mesh axis runs over, the one named last changes fastest.
Arguments:
- inputs: bfloat16 [128, 128, 32768], P('block', None, 'dp'), may hold values from -6 to 6
- left_factor: bfloat16 [128, 128, 128], P('block'), may hold values from -0.5 to 0.5
- right_factor: bfloat16 [128, 128, 128], P('block'), may hold values from -0.5 to 0.5
- cotangent: bfloat16 [128, 128, 32768], P('block', None, 'dp'), may hold values from -6 to 6
Outputs:
- input_grad: bfloat16 [128, 128, 32768], P('block', None, 'dp')
- left_grad: float32 [128, 128, 128], P('block', 'dp')
- right_grad: float32 [128, 128, 128], P('block', 'dp')
All inputs are finite; a program needn't handle non-finite values.
Results may differ from a plain program's by a relative error of at most 0.0055.
Values may be sent and summed in bfloat16 or wider, within the bound.
No kernel may reach another device: no remote copies, remote signals or barrier semaphores. Data moves between devices by JAX's collectives and lax.ppermute only.
A program may use at most 128 MiB of HBM per device.

v0:
```python
import jax
import jax.numpy as jnp
from jax import lax
from jax.sharding import PartitionSpec as P

CHUNKS = (13, 3)
SPLIT_DP = False


def gelu_slope(values):
    return jax.vjp(jax.nn.gelu, values)[1](jnp.ones_like(values))[0]


def dp_reduce_scatter(terms):
    n_dp = lax.axis_size("dp")
    received = lax.all_to_all(terms, "dp", split_axis=2, concat_axis=0, tiled=True)
    received = received.reshape(
        (n_dp,) + terms.shape[:2] + (terms.shape[2] // n_dp,) + terms.shape[3:]
    )
    return jnp.sum(received, axis=0)


def local(inputs, left_factor, right_factor, cotangent):
    tokens_local = inputs.shape[2]
    scale = float(lax.axis_size("dp") * tokens_local) ** (-0.5)
    total = sum(CHUNKS)
    bounds = [0]
    for share in CHUNKS:
        bounds.append(bounds[-1] + tokens_local * share // total)
    input_pieces = []
    grad_left = None
    grad_right = None
    right_done = None
    for group in range(len(CHUNKS)):
        lo, hi = (bounds[group], bounds[group + 1])
        x_group = inputs[:, :, lo:hi]
        dy_group = cotangent[:, :, lo:hi]
        outgoing = jnp.einsum(
            "ict,ico->oit", x_group, left_factor, preferred_element_type=jnp.float32
        ).astype(jnp.bfloat16)
        forward_received = lax.all_to_all(
            outgoing, "block", split_axis=0, concat_axis=1, tiled=True
        )
        mixed = jnp.einsum(
            "jit,jik->jkt", forward_received, right_factor, preferred_element_type=jnp.float32
        )
        slope = gelu_slope(mixed)
        mixed_grad = (dy_group.astype(jnp.float32) * slope).astype(jnp.bfloat16)
        right_term = (
            jnp.einsum(
                "jit,jkt->jik", forward_received, mixed_grad, preferred_element_type=jnp.float32
            )
            * scale
        )
        grad_right = right_term if grad_right is None else grad_right + right_term
        if SPLIT_DP and group == len(CHUNKS) - 1:
            right_done = dp_reduce_scatter(grad_right[None])[0]
        permuted_grad = jnp.einsum(
            "jkt,jik->jit", mixed_grad, right_factor, preferred_element_type=jnp.float32
        ).astype(jnp.bfloat16)
        received = lax.all_to_all(permuted_grad, "block", split_axis=1, concat_axis=0, tiled=True)
        branch = jnp.einsum(
            "oit,ico->ict", received, left_factor, preferred_element_type=jnp.float32
        )
        residual = dy_group.astype(jnp.float32)
        input_pieces.append((residual + branch).astype(jnp.bfloat16))
        left_term = (
            jnp.einsum("ict,oit->ico", x_group, received, preferred_element_type=jnp.float32)
            * scale
        )
        grad_left = left_term if grad_left is None else grad_left + left_term
    input_grad = jnp.concatenate(input_pieces, axis=2)
    if SPLIT_DP:
        return (input_grad, dp_reduce_scatter(grad_left[None])[0], right_done)
    reduced = dp_reduce_scatter(jnp.stack([grad_left, grad_right]))
    return (input_grad, reduced[0], reduced[1])


def solution(mesh):
    placed = (
        P("block", None, "dp"),
        P("block", None, None),
        P("block", None, None),
        P("block", None, "dp"),
    )
    return jax.shard_map(
        local,
        mesh=mesh,
        in_specs=placed,
        out_specs=(P("block", None, "dp"), P("block", "dp", None), P("block", "dp", None)),
        check_vma=False,
    )
```

profile of v0, /device:TPU:1, one launch (start us, length us, event | category | flops | bytes accessed | tf_op | source)
XLA Modules:
  0.0 259.9 jit_solution(1413870222509505531)
XLA Ops:
  0.7 1.7 fusion.30
  3.7 10.0 %all-to-all-start.2 = ((bf16[128,8,384]{2,1,0:T(8,128)(2,1)}), bf16[128,8,384]{2,1,0:T(8,128)(2,1)S(1)}, u32[]{:S(2)}, u32[]{:S(2)}) async-start(bf16[128,8,384]{2,1,0:T(8,128)(2,1)} %copy.85), calls=%async_computation.2 | async-start | bytes 1572864 | tf_op jit(solution)/shard_map/all_to_all | solution.py:41
  13.7 3.1 %fusion.12 = bf16[128,8,1664]{2,0,1:T(8,128)(2,1)S(1)} fusion(bf16[8,128,128]{2,1,0:T(8,128)(2,1)S(1)} %copy-done.4, bf16[8,128,2048]{2,1,0:T(8,128)(2,1)} %param.4), kind=kOutput, calls=%fused_computation.20 | convolution fusion | flops 437911552 | bytes 7077888 | tf_op jit(solution)/shard_map/ict,ico->oit/dot_general | solution.py:38
  16.8 3.7 %copy.76 = bf16[128,8,1664]{2,1,0:T(8,128)(2,1)} copy(bf16[128,8,1664]{2,0,1:T(8,128)(2,1)S(1)} %fusion.12) | data formatting | bytes 6815744 | tf_op jit(solution)/shard_map/convert_element_type | solution.py:40
  20.5 14.0 %all-to-all-done.2 = bf16[128,8,384]{2,1,0:T(8,128)(2,1)S(1)} async-done(((bf16[128,8,384]{2,1,0:T(8,128)(2,1)}), bf16[128,8,384]{2,1,0:T(8,128)(2,1)S(1)}, u32[]{:S(2)}, u32[]{:S(2)}) %all-to-all-start.2) | async-done | bytes 786464 | tf_op jit(solution)/shard_map/all_to_all | solution.py:41
  35.4 5.3 %all-to-all-start = ((bf16[128,8,1664]{2,1,0:T(8,128)(2,1)}), bf16[128,8,1664]{2,1,0:T(8,128)(2,1)}, u32[]{:S(2)}, u32[]{:S(2)}) async-start(bf16[128,8,1664]{2,1,0:T(8,128)(2,1)} %copy.76), calls=%async_computation | async-start | bytes 6815744 | tf_op jit(solution)/shard_map/all_to_all | solution.py:41
  40.7 4.1 %slice.18 = bf16[8,128,1664]{2,1,0:T(8,128)(2,1)} slice(bf16[8,128,2048]{2,1,0:T(8,128)(2,1)} %param.7), slice={[0:8], [0:128], [0:1664]} | slice | bytes 6815744 | tf_op jit(solution)/shard_map/slice | solution.py:37
  45.2 5.9 %copy.113 = bf16[8,128,1664]{1,2,0:T(8,128)(2,1)} copy(bf16[8,128,1664]{2,1,0:T(8,128)(2,1)} %slice.18) | data formatting | bytes 6815744
  54.1 64.7 %all-to-all-done = bf16[128,8,1664]{2,1,0:T(8,128)(2,1)} async-done(((bf16[128,8,1664]{2,1,0:T(8,128)(2,1)}), bf16[128,8,1664]{2,1,0:T(8,128)(2,1)}, u32[]{:S(2)}, u32[]{:S(2)}) %all-to-all-start) | async-done | bytes 3407904 | tf_op jit(solution)/shard_map/all_to_all | solution.py:41
  118.9 4.1 %all-to-all-start.3 = ((bf16[8,128,384]{2,0,1:T(8,128)(2,1)}), bf16[8,128,384]{2,0,1:T(8,128)(2,1)S(1)}, u32[]{:S(2)}, u32[]{:S(2)}) async-start(bf16[8,128,384]{2,0,1:T(8,128)(2,1)} %copy.88), calls=%async_computation.3 | async-start | bytes 1572864 | tf_op jit(solution)/shard_map/all_to_all | solution.py:61
  123.0 7.6 %fusion = bf16[8,128,1664]{1,2,0:T(8,128)(2,1)S(1)} fusion(bf16[8,128,1664]{1,2,0:T(8,128)(2,1)} %copy.113, bf16[8,128,128]{2,1,0:T(8,128)(2,1)S(1)} %copy-done, bf16[8,16,8,1664]{3,2,0,1:T(8,128)(2,1)} %bitcast.2), kind=kOutput, calls=%fused_computation.4 | convolution fusion | flops 470286336 | bytes 10485760 | tf_op jit(solution)/shard_map/jit,jik->jkt/dot_general | solution.py:44
  130.6 1.7 copy-done.5
  132.3 2.8 %fusion.13 = bf16[8,128,1664]{1,2,0:T(8,128)(2,1)} fusion(bf16[8,128,1664]{1,2,0:T(8,128)(2,1)S(1)} %fusion, bf16[8,128,128]{2,1,0:T(8,128)(2,1)S(1)} %copy-done), kind=kOutput, calls=%fused_computation.21 | convolution fusion | flops 437911552 | bytes 7077888 | tf_op jit(solution)/shard_map/jkt,jik->jit/dot_general | solution.py:58
  135.1 6.0 %copy.79 = bf16[8,128,1664]{2,0,1:T(8,128)(2,1)} copy(bf16[8,128,1664]{1,2,0:T(8,128)(2,1)} %fusion.13) | data formatting | bytes 6815744 | tf_op jit(solution)/shard_map/convert_element_type | solution.py:60
  141.0 2.5 all-to-all-done.3
  143.5 5.5 %all-to-all-start.1 = ((bf16[8,128,1664]{2,0,1:T(8,128)(2,1)}), bf16[8,128,1664]{2,0,1:T(8,128)(2,1)}, u32[]{:S(2)}, u32[]{:S(2)}) async-start(bf16[8,128,1664]{2,0,1:T(8,128)(2,1)} %copy.79), calls=%async_computation.1 | async-start | bytes 6815744 | tf_op jit(solution)/shard_map/all_to_all | solution.py:61
  149.2 4.3 %fusion.9 = f32[8,128,128]{1,2,0:T(8,128)S(1)} fusion(bf16[8,128,1664]{1,2,0:T(8,128)(2,1)} %copy-done.5, bf16[8,16,8,1664]{3,2,0,1:T(8,128)(2,1)} %bitcast.2), kind=kOutput, calls=%fused_computation.17 | convolution fusion | flops 436207616 | bytes 7340032 | tf_op jit(solution)/shard_map/jit,jkt->jik/dot_general | solution.py:50
  154.8 72.4 %all-to-all-done.1 = bf16[8,128,1664]{2,0,1:T(8,128)(2,1)} async-done(((bf16[8,128,1664]{2,0,1:T(8,128)(2,1)}), bf16[8,128,1664]{2,0,1:T(8,128)(2,1)}, u32[]{:S(2)}, u32[]{:S(2)}) %all-to-all-start.1) | async-done | bytes 3407904 | tf_op jit(solution)/shard_map/all_to_all | solution.py:61
  227.3 2.6 %copy.81 = bf16[16,8,8,1664]{3,2,1,0:T(8,128)(2,1)S(1)} copy(bf16[16,8,8,1664]{3,1,2,0:T(8,128)(2,1)} %bitcast.8) | data formatting | bytes 6815744 | tf_op jit(solution)/shard_map/all_to_all | solution.py:61
  233.7 8.4 %all-to-all-start.4 = ((f32[2,8,128,128]{3,1,0,2:T(8,128)}), f32[2,8,128,128]{3,1,0,2:T(8,128)S(1)}, u32[]{:S(2)}, u32[]{:S(2)}) async-start(f32[2,8,128,128]{3,1,0,2:T(8,128)} %copy.99), calls=%async_computation.4 | async-start | bytes 2097152 | tf_op jit(solution)/shard_map/all_to_all | solution.py:16
  242.6 4.7 %fusion.1 = bf16[8,128,1664]{1,2,0:T(8,128)(2,1)S(1)} fusion(bf16[8,128,1664]{1,2,0:T(8,128)(2,1)} %copy.113, bf16[8,128,128]{2,1,0:T(8,128)(2,1)S(1)} %copy-done.4, bf16[128,8,1664]{2,1,0:T(8,128)(2,1)} %bitcast.82), kind=kOutput, calls=%fused_computation.5 | convolution fusion | flops 441319424 | bytes 10485760 | tf_op jit(solution)/shard_map/oit,ico->ict/dot_general | solution.py:62
  247.3 2.2 pad_maximum_fusion
  249.5 6.4 %copy.101 = bf16[8,128,2048]{2,1,0:T(8,128)(2,1)} copy(bf16[8,128,2048]{1,2,0:T(8,128)(2,1)} %pad_maximum_fusion) | data formatting | bytes 8388608
  256.0 3.3 %all-to-all-done.4 = f32[2,8,128,128]{3,1,0,2:T(8,128)S(1)} async-done(((f32[2,8,128,128]{3,1,0,2:T(8,128)}), f32[2,8,128,128]{3,1,0,2:T(8,128)S(1)}, u32[]{:S(2)}, u32[]{:S(2)}) %all-to-all-start.4) | async-done | bytes 1048608 | tf_op jit(solution)/shard_map/all_to_all | solution.py:16
  (40 shorter events, 12.0 us)
Async XLA Ops:
  0.6 50.4 %copy-start = (bf16[8,128,128]{2,1,0:T(8,128)(2,1)S(1)}, bf16[8,128,128]{2,1,0:T(8,128)(2,1)}, u32[]{:S(2)}) copy-start(bf16[8,128,128]{2,1,0:T(8,128)(2,1)} %param.6) | copy-start | bytes 786436
  0.6 13.1 %copy-start.4 = (bf16[8,128,128]{2,1,0:T(8,128)(2,1)S(1)}, bf16[8,128,128]{2,1,0:T(8,128)(2,1)}, u32[]{:S(2)}) copy-start(bf16[8,128,128]{2,1,0:T(8,128)(2,1)} %param.5) | copy-start | bytes 786436
  3.7 30.8 %all-to-all-start.2 = ((bf16[128,8,384]{2,1,0:T(8,128)(2,1)}), bf16[128,8,384]{2,1,0:T(8,128)(2,1)S(1)}, u32[]{:S(2)}, u32[]{:S(2)}) async-start(bf16[128,8,384]{2,1,0:T(8,128)(2,1)} %copy.85), calls=%async_computation.2 | async-start | bytes 1572864 | tf_op jit(solution)/shard_map/all_to_all | solution.py:41
  34.5 0.9 copy-start.8
  35.4 83.5 %all-to-all-start = ((bf16[128,8,1664]{2,1,0:T(8,128)(2,1)}), bf16[128,8,1664]{2,1,0:T(8,128)(2,1)}, u32[]{:S(2)}, u32[]{:S(2)}) async-start(bf16[128,8,1664]{2,1,0:T(8,128)(2,1)} %copy.76), calls=%async_computation | async-start | bytes 6815744 | tf_op jit(solution)/shard_map/all_to_all | solution.py:41
  40.7 4.1 %slice-start = ((bf16[8,128,2048]{2,1,0:T(8,128)(2,1)}), bf16[8,128,384]{2,1,0:T(8,128)(2,1)S(1)}, s32[]{:S(2)}) async-start(bf16[8,128,2048]{2,1,0:T(8,128)(2,1)} %param.7), calls=%async_computation.5 | async-start | bytes 1572864 | tf_op jit(solution)/shard_map/slice | solution.py:37
  45.2 5.9 %copy-start.6 = (bf16[8,128,384]{1,2,0:T(8,128)(2,1)}, bf16[8,128,384]{1,2,0:T(8,128)(2,1)S(1)}, u32[]{:S(2)}) copy-start(bf16[8,128,384]{1,2,0:T(8,128)(2,1)S(1)} %copy.114) | copy-start | bytes 2359300
  45.2 5.9 %copy-start.9 = (bf16[128,8,384]{2,1,0:T(8,128)(2,1)S(1)}, bf16[128,8,384]{2,1,0:T(8,128)(2,1)}, u32[]{:S(2)}) copy-start(bf16[128,8,384]{2,1,0:T(8,128)(2,1)} %copy-done.8) | copy-start | bytes 2359300
  118.9 24.7 %all-to-all-start.3 = ((bf16[8,128,384]{2,0,1:T(8,128)(2,1)}), bf16[8,128,384]{2,0,1:T(8,128)(2,1)S(1)}, u32[]{:S(2)}, u32[]{:S(2)}) async-start(bf16[8,128,384]{2,0,1:T(8,128)(2,1)} %copy.88), calls=%async_computation.3 | async-start | bytes 1572864 | tf_op jit(solution)/shard_map/all_to_all | solution.py:61
  130.6 1.7 copy-start.5
  143.5 83.7 %all-to-all-start.1 = ((bf16[8,128,1664]{2,0,1:T(8,128)(2,1)}), bf16[8,128,1664]{2,0,1:T(8,128)(2,1)}, u32[]{:S(2)}, u32[]{:S(2)}) async-start(bf16[8,128,1664]{2,0,1:T(8,128)(2,1)} %copy.79), calls=%async_computation.1 | async-start | bytes 6815744 | tf_op jit(solution)/shard_map/all_to_all | solution.py:61
  149.2 4.3 %copy-start.10 = (bf16[128,8,384]{2,1,0:T(8,128)(2,1)S(1)}, bf16[128,8,384]{2,1,0:T(8,128)(2,1)}, u32[]{:S(2)}) copy-start(bf16[128,8,384]{2,1,0:T(8,128)(2,1)} %copy-done.8) | copy-start | bytes 2359300
  227.3 3.2 %copy-start.3 = (bf16[8,128,2048]{2,1,0:T(8,128)(2,1)S(1)}, bf16[8,128,2048]{2,1,0:T(8,128)(2,1)}, u32[]{:S(2)}) copy-start(bf16[8,128,2048]{2,1,0:T(8,128)(2,1)} %param.4) | copy-start | bytes 12582916
  229.9 1.8 copy-start.2
  230.5 1.7 copy-start.11
  232.2 9.9 %copy-start.7 = (bf16[8,128,384]{1,2,0:T(8,128)(2,1)S(1)}, bf16[8,128,384]{1,2,0:T(8,128)(2,1)}, u32[]{:S(2)}) copy-start(bf16[8,128,384]{1,2,0:T(8,128)(2,1)} %copy-done.6) | copy-start | bytes 2359300
  233.7 25.5 %all-to-all-start.4 = ((f32[2,8,128,128]{3,1,0,2:T(8,128)}), f32[2,8,128,128]{3,1,0,2:T(8,128)S(1)}, u32[]{:S(2)}, u32[]{:S(2)}) async-start(f32[2,8,128,128]{3,1,0,2:T(8,128)} %copy.99), calls=%async_computation.4 | async-start | bytes 2097152 | tf_op jit(solution)/shard_map/all_to_all | solution.py:16
  247.3 12.7 %copy-start.1 = (bf16[8,128,128]{2,1,0:T(8,128)(2,1)S(1)}, bf16[8,128,128]{2,1,0:T(8,128)(2,1)}, u32[]{:S(2)}) copy-start(bf16[8,128,128]{2,1,0:T(8,128)(2,1)} %param.6) | copy-start | bytes 786436
where the time goes:
time: 261 us; the launch traced here: 260 us
  waiting for transfers between devices  157 us (60%)
  local copies, waits for them, and re-layouts  37 us (14%)
  starting transfers between devices  33.5 us (13%)
  matrix products  29.2 us (11%)
    all_to_all x2, waiting for transfers between devices, local(): lax.all_to_all(outgoing, 'block', split_axis=0, concat_axis=1, tiled=True)  78.8 us
    all_to_all x2, waiting for transfers between devices, local(): lax.all_to_all(permuted_grad, 'block', split_axis=1, concat_axis=0, tiled...  74.9 us
    unnamed x27, local copies, waits for them, and re-layouts  15.9 us
    all_to_all x2, starting transfers between devices, local(): lax.all_to_all(outgoing, 'block', split_axis=0, concat_axis=1, tiled=True)  15.4 us
    all_to_all x2, starting transfers between devices, local(): lax.all_to_all(permuted_grad, 'block', split_axis=1, concat_axis=0, tiled...  9.67 us
    dot_general x2, matrix products, local(): jnp.einsum('jit,jik->jkt', forward_received, right_factor, preferred_elem...  8.9 us
    all_to_all x1, starting transfers between devices, dp_reduce_scatter(): lax.all_to_all(terms, 'dp', split_axis=2, concat_axis=0, tiled=True)  8.45 us
    convert_element_type x2, local copies, waits for them, and re-layouts, local(): permuted_grad = jnp.einsum('jkt,jik->jit', mixed_grad, right_factor, pref...  7.3 us
  transfers between devices with their start and end apart: 5, of which 5 were waited for; matrix products, arithmetic and copies ran while one was open for 22% of the time, Pallas kernels for 0%

commit v1 on v0

--- a/solution.py
+++ b/solution.py
@@ -58,7 +58,12 @@
         permuted_grad = jnp.einsum(
             "jkt,jik->jit", mixed_grad, right_factor, preferred_element_type=jnp.float32
         ).astype(jnp.bfloat16)
-        received = lax.all_to_all(permuted_grad, "block", split_axis=1, concat_axis=0, tiled=True)
+        received = jnp.concatenate(
+            lax.all_to_all(
+                jnp.stack(jnp.split(permuted_grad, lax.axis_size("block"), axis=1)), "block", 0, 0
+            ),
+            axis=0,
+        )
         branch = jnp.einsum(
             "oit,ico->ict", received, left_factor, preferred_element_type=jnp.float32
         )

time: 261 us -> 265 us (1.015)
  waiting for transfers between devices: 157 us -> 154 us
  starting transfers between devices: 33.5 us -> 36.3 us
  matrix products: 29.2 us -> 31.9 us
    all_to_all x2, waiting for transfers between devices: 78.8 us -> 66.3 us  [local(): lax.all_to_all(outgoing, 'block', split_axis=0, concat_axis=1, tiled=True)]
    all_to_all x2, waiting for transfers between devices: 74.9 us -> 84.5 us  [local(): lax.all_to_all(jnp.stack(jnp.split(permuted_grad, lax.axis_size('block'),...]
    unnamed x27 -> x45, local copies, waits for them, and re-layouts: 15.9 us -> 25.5 us
    convert_element_type x2 -> x0, local copies, waits for them, and re-layouts: 7.3 us -> none  [local(): permuted_grad = jnp.einsum('jkt,jik->jit', mixed_grad, right_factor, pref...]
    dot_general x2, matrix products: 1.69 us -> 4.76 us  [local(): jnp.einsum('ict,oit->ico', x_group, received, preferred_element_type=jnp....]
    all_to_all x2 -> x0, local copies, waits for them, and re-layouts: 2.76 us -> none  [local(): lax.all_to_all(permuted_grad, 'block', split_axis=1, concat_axis=0, tiled...]
  transfers between devices with their start and end apart: 5 -> 5, of which waited for: 5 -> 4; matrix products, arithmetic and copies ran while one was open for 22% -> 22% of each run, Pallas kernels for 0% -> 0%
where the time goes in v1:
time: 265 us; the launch traced here: 264 us
  waiting for transfers between devices  154 us (58%)
  local copies, waits for them, and re-layouts  37.2 us (14%)
  starting transfers between devices  36.3 us (14%)
  matrix products  31.9 us (12%)
  other arithmetic  3.52 us (1%)
    all_to_all x2, waiting for transfers between devices, local(): lax.all_to_all(jnp.stack(jnp.split(permuted_grad, lax.axis_size('block'),...  84.5 us
    all_to_all x2, waiting for transfers between devices, local(): lax.all_to_all(outgoing, 'block', split_axis=0, concat_axis=1, tiled=True)  66.3 us
    unnamed x45, local copies, waits for them, and re-layouts  25.5 us
    all_to_all x2, starting transfers between devices, local(): lax.all_to_all(outgoing, 'block', split_axis=0, concat_axis=1, tiled=True)  14.2 us
    all_to_all x2, starting transfers between devices, local(): lax.all_to_all(jnp.stack(jnp.split(permuted_grad, lax.axis_size('block'),...  11.8 us
    all_to_all x1, starting transfers between devices, dp_reduce_scatter(): lax.all_to_all(terms, 'dp', split_axis=2, concat_axis=0, tiled=True)  10.2 us
    dot_general x2, matrix products, local(): jnp.einsum('jit,jik->jkt', forward_received, right_factor, preferred_elem...  10 us
    dot_general x2, matrix products, local(): jnp.einsum('jit,jkt->jik', forward_received, mixed_grad, preferred_elemen...  5.65 us
  transfers between devices with their start and end apart: 5, of which 4 were waited for; matrix products, arithmetic and copies ran while one was open for 22% of the time, Pallas kernels for 0%

profile of v1, /device:TPU:1, one launch (start us, length us, event | category | flops | bytes accessed | tf_op | source)
XLA Modules:
  0.0 263.9 jit_solution(8018607564177083228)
XLA Ops:
  0.6 3.2 %fusion.12 = bf16[128,8,1664]{2,0,1:T(8,128)(2,1)S(1)} fusion(bf16[8,128,128]{2,1,0:T(8,128)(2,1)} %param.5, bf16[8,128,2048]{2,1,0:T(8,128)(2,1)} %param.4), kind=kOutput, calls=%fused_computation.20 | convolution fusion | flops 437911552 | bytes 7077888 | tf_op jit(solution)/shard_map/ict,ico->oit/dot_general | solution.py:38
  3.8 3.7 %copy.72 = bf16[128,8,1664]{2,1,0:T(8,128)(2,1)} copy(bf16[128,8,1664]{2,0,1:T(8,128)(2,1)S(1)} %fusion.12) | data formatting | bytes 6815744 | tf_op jit(solution)/shard_map/convert_element_type | solution.py:40
  7.5 10.2 %all-to-all-start = ((bf16[128,8,1664]{2,1,0:T(8,128)(2,1)}), bf16[128,8,1664]{2,1,0:T(8,128)(2,1)}, u32[]{:S(2)}, u32[]{:S(2)}) async-start(bf16[128,8,1664]{2,1,0:T(8,128)(2,1)} %copy.72), calls=%async_computation | async-start | bytes 6815744 | tf_op jit(solution)/shard_map/all_to_all | solution.py:41
  17.7 1.5 fusion.30
  19.3 1.4 copy.79
  20.7 4.0 %slice.18 = bf16[8,128,1664]{2,1,0:T(8,128)(2,1)} slice(bf16[8,128,2048]{2,1,0:T(8,128)(2,1)} %param.7), slice={[0:8], [0:128], [0:1664]} | slice | bytes 6815744 | tf_op jit(solution)/shard_map/slice | solution.py:37
  24.6 5.6 %copy.105 = bf16[8,128,1664]{1,2,0:T(8,128)(2,1)} copy(bf16[8,128,1664]{2,1,0:T(8,128)(2,1)} %slice.18) | data formatting | bytes 6815744
  30.2 66.3 %all-to-all-done = bf16[128,8,1664]{2,1,0:T(8,128)(2,1)} async-done(((bf16[128,8,1664]{2,1,0:T(8,128)(2,1)}), bf16[128,8,1664]{2,1,0:T(8,128)(2,1)}, u32[]{:S(2)}, u32[]{:S(2)}) %all-to-all-start) | async-done | bytes 3407904 | tf_op jit(solution)/shard_map/all_to_all | solution.py:41
  96.5 4.0 %all-to-all-start.2 = ((bf16[128,8,384]{2,1,0:T(8,128)(2,1)}), bf16[128,8,384]{2,1,0:T(8,128)(2,1)S(1)}, u32[]{:S(2)}, u32[]{:S(2)}) async-start(bf16[128,8,384]{2,1,0:T(8,128)(2,1)} %copy.79), calls=%async_computation.2 | async-start | bytes 1572864 | tf_op jit(solution)/shard_map/all_to_all | solution.py:41
  100.6 7.6 %fusion = bf16[8,128,1664]{1,2,0:T(8,128)(2,1)S(1)} fusion(bf16[8,128,1664]{1,2,0:T(8,128)(2,1)} %copy.105, bf16[8,128,128]{2,1,0:T(8,128)(2,1)S(1)} %copy-done, bf16[8,16,8,1664]{3,2,0,1:T(8,128)(2,1)} %bitcast.2), kind=kOutput, calls=%fused_computation.4 | convolution fusion | flops 470286336 | bytes 10485760 | tf_op jit(solution)/shard_map/jit,jik->jkt/dot_general | solution.py:44
  121.2 7.7 %all-to-all-start.1 = ((bf16[16,8,8,1664]{3,2,1,0:T(8,128)(2,1)}), bf16[16,8,8,1664]{3,2,1,0:T(8,128)(2,1)}, u32[]{:S(2)}, u32[]{:S(2)}) async-start(bf16[16,8,8,1664]{3,2,1,0:T(8,128)(2,1)} %fusion.44), calls=%async_computation.1 | async-start | bytes 6815744 | tf_op jit(solution)/shard_map/all_to_all | solution.py:62
  130.1 2.5 fusion.21
  134.3 72.8 %all-to-all-done.1 = bf16[16,8,8,1664]{3,2,1,0:T(8,128)(2,1)} async-done(((bf16[16,8,8,1664]{3,2,1,0:T(8,128)(2,1)}), bf16[16,8,8,1664]{3,2,1,0:T(8,128)(2,1)}, u32[]{:S(2)}, u32[]{:S(2)}) %all-to-all-start.1) | async-done | bytes 3407904 | tf_op jit(solution)/shard_map/all_to_all | solution.py:62
  207.1 4.1 %all-to-all-start.3 = ((bf16[16,8,8,384]{3,2,1,0:T(8,128)(2,1)}), bf16[16,8,8,384]{3,2,1,0:T(8,128)(2,1)S(1)}, u32[]{:S(2)}, u32[]{:S(2)}) async-start(bf16[16,8,8,384]{3,2,1,0:T(8,128)(2,1)} %copy-done.5), calls=%async_computation.3 | async-start | bytes 1572864 | tf_op jit(solution)/shard_map/all_to_all | solution.py:62
  211.2 4.4 %fusion.9 = f32[8,128,128]{1,2,0:T(8,128)S(1)} fusion(bf16[8,128,1664]{1,2,0:T(8,128)(2,1)} %copy-done.3, bf16[8,16,8,1664]{3,2,0,1:T(8,128)(2,1)} %bitcast.2), kind=kOutput, calls=%fused_computation.17 | convolution fusion | flops 436207616 | bytes 7340032 | tf_op jit(solution)/shard_map/jit,jkt->jik/dot_general | solution.py:50
  216.9 3.2 %fusion.15 = f32[8,128,128]{2,1,0:T(8,128)S(1)} fusion(bf16[128,8,1664]{2,1,0:T(8,128)(2,1)} %bitcast.22, bf16[8,128,2048]{2,1,0:T(8,128)(2,1)S(1)} %copy-done.1), kind=kOutput, calls=%fused_computation.23 | convolution fusion | flops 436207616 | bytes 7340032 | tf_op jit(solution)/shard_map/ict,oit->ico/dot_general | solution.py:73
  220.0 11.7 %all-to-all-done.3 = bf16[16,8,8,384]{3,2,1,0:T(8,128)(2,1)S(1)} async-done(((bf16[16,8,8,384]{3,2,1,0:T(8,128)(2,1)}), bf16[16,8,8,384]{3,2,1,0:T(8,128)(2,1)S(1)}, u32[]{:S(2)}, u32[]{:S(2)}) %all-to-all-start.3) | async-done | bytes 786464 | tf_op jit(solution)/shard_map/all_to_all | solution.py:62
  231.7 1.6 fusion.33
  234.5 1.4 copy.91
  235.9 10.2 %all-to-all-start.4 = ((f32[2,8,128,128]{3,1,0,2:T(8,128)}), f32[2,8,128,128]{3,1,0,2:T(8,128)S(1)}, u32[]{:S(2)}, u32[]{:S(2)}) async-start(f32[2,8,128,128]{3,1,0,2:T(8,128)} %copy.91), calls=%async_computation.4 | async-start | bytes 2097152 | tf_op jit(solution)/shard_map/all_to_all | solution.py:16
  246.5 4.7 %fusion.1 = bf16[8,128,1664]{1,2,0:T(8,128)(2,1)S(1)} fusion(bf16[8,128,1664]{1,2,0:T(8,128)(2,1)} %copy.105, bf16[8,128,128]{2,1,0:T(8,128)(2,1)S(1)} %copy-done.2, bf16[128,8,1664]{2,1,0:T(8,128)(2,1)} %bitcast.22), kind=kOutput, calls=%fused_computation.5 | convolution fusion | flops 441319424 | bytes 10485760 | tf_op jit(solution)/shard_map/oit,ico->ict/dot_general | solution.py:67
  251.2 2.3 pad_maximum_fusion
  253.5 6.4 %copy.93 = bf16[8,128,2048]{2,1,0:T(8,128)(2,1)} copy(bf16[8,128,2048]{1,2,0:T(8,128)(2,1)} %pad_maximum_fusion) | data formatting | bytes 8388608
  259.9 3.2 %all-to-all-done.4 = f32[2,8,128,128]{3,1,0,2:T(8,128)S(1)} async-done(((f32[2,8,128,128]{3,1,0,2:T(8,128)}), f32[2,8,128,128]{3,1,0,2:T(8,128)S(1)}, u32[]{:S(2)}, u32[]{:S(2)}) %all-to-all-start.4) | async-done | bytes 1048608 | tf_op jit(solution)/shard_map/all_to_all | solution.py:16
  (56 shorter events, 19.4 us)
Async XLA Ops:
  0.6 99.9 %copy-start = (bf16[8,128,128]{2,1,0:T(8,128)(2,1)S(1)}, bf16[8,128,128]{2,1,0:T(8,128)(2,1)}, u32[]{:S(2)}) copy-start(bf16[8,128,128]{2,1,0:T(8,128)(2,1)} %param.6) | copy-start | bytes 786436
  7.5 10.2 %copy-start.2 = (bf16[8,128,128]{2,1,0:T(8,128)(2,1)S(1)}, bf16[8,128,128]{2,1,0:T(8,128)(2,1)}, u32[]{:S(2)}) copy-start(bf16[8,128,128]{2,1,0:T(8,128)(2,1)} %param.5) | copy-start | bytes 786436
  7.5 89.0 %all-to-all-start = ((bf16[128,8,1664]{2,1,0:T(8,128)(2,1)}), bf16[128,8,1664]{2,1,0:T(8,128)(2,1)}, u32[]{:S(2)}, u32[]{:S(2)}) async-start(bf16[128,8,1664]{2,1,0:T(8,128)(2,1)} %copy.72), calls=%async_computation | async-start | bytes 6815744 | tf_op jit(solution)/shard_map/all_to_all | solution.py:41
  96.5 24.7 %all-to-all-start.2 = ((bf16[128,8,384]{2,1,0:T(8,128)(2,1)}), bf16[128,8,384]{2,1,0:T(8,128)(2,1)S(1)}, u32[]{:S(2)}, u32[]{:S(2)}) async-start(bf16[128,8,384]{2,1,0:T(8,128)(2,1)} %copy.79), calls=%async_computation.2 | async-start | bytes 1572864 | tf_op jit(solution)/shard_map/all_to_all | solution.py:41
  108.1 1.9 copy-start.3
  121.2 7.8 %slice-start = ((bf16[8,128,2048]{2,1,0:T(8,128)(2,1)}), bf16[8,128,384]{2,1,0:T(8,128)(2,1)S(1)}, s32[]{:S(2)}) async-start(bf16[8,128,2048]{2,1,0:T(8,128)(2,1)} %param.7), calls=%async_computation.5 | async-start | bytes 1572864 | tf_op jit(solution)/shard_map/slice | solution.py:37
  121.2 85.9 %all-to-all-start.1 = ((bf16[16,8,8,1664]{3,2,1,0:T(8,128)(2,1)}), bf16[16,8,8,1664]{3,2,1,0:T(8,128)(2,1)}, u32[]{:S(2)}, u32[]{:S(2)}) async-start(bf16[16,8,8,1664]{3,2,1,0:T(8,128)(2,1)} %fusion.44), calls=%async_computation.1 | async-start | bytes 6815744 | tf_op jit(solution)/shard_map/all_to_all | solution.py:62
  133.4 0.9 copy-start.5
  207.1 24.6 %all-to-all-start.3 = ((bf16[16,8,8,384]{3,2,1,0:T(8,128)(2,1)}), bf16[16,8,8,384]{3,2,1,0:T(8,128)(2,1)S(1)}, u32[]{:S(2)}, u32[]{:S(2)}) async-start(bf16[16,8,8,384]{3,2,1,0:T(8,128)(2,1)} %copy-done.5), calls=%async_computation.3 | async-start | bytes 1572864 | tf_op jit(solution)/shard_map/all_to_all | solution.py:62
  211.2 5.7 %copy-start.1 = (bf16[8,128,2048]{2,1,0:T(8,128)(2,1)S(1)}, bf16[8,128,2048]{2,1,0:T(8,128)(2,1)}, u32[]{:S(2)}) copy-start(bf16[8,128,2048]{2,1,0:T(8,128)(2,1)} %param.4) | copy-start | bytes 12582916
  233.3 12.8 %copy-start.4 = (bf16[8,128,384]{1,2,0:T(8,128)(2,1)S(1)}, bf16[8,128,384]{1,2,0:T(8,128)(2,1)}, u32[]{:S(2)}) copy-start(bf16[8,128,384]{1,2,0:T(8,128)(2,1)} %copy.106) | copy-start | bytes 2359300
  235.9 27.3 %all-to-all-start.4 = ((f32[2,8,128,128]{3,1,0,2:T(8,128)}), f32[2,8,128,128]{3,1,0,2:T(8,128)S(1)}, u32[]{:S(2)}, u32[]{:S(2)}) async-start(f32[2,8,128,128]{3,1,0,2:T(8,128)} %copy.91), calls=%async_computation.4 | async-start | bytes 2097152 | tf_op jit(solution)/shard_map/all_to_all | solution.py:16
